TPU v7x, 256 devices: a whole 4x4x8 slice. The times are simulated.
256 devices in a mesh: seq: 64 (over z_hi, y, x, core), tp: 4 (over z_lo).
Axes of the slice: x: 4, y: 4, z: 8 (z_hi: 2, z_lo: 4; z = z_hi * 4 + z_lo), core: 2. Of those that a mesh axis runs over, the one named last changes fastest.
Arguments:
- residual: bfloat16 [32768, 2048], P('seq', 'tp'), may hold values from -6 to 6
- norm_gain: float32 [2048], replicated, may hold values from 0.3 to 3
- query_weight: bfloat16 [2048, 1024], P(None, 'tp'), as said below
- key_weight: bfloat16 [2048, 1024], P(None, 'tp'), as said below
- value_weight: bfloat16 [2048, 1024], P(None, 'tp'), may hold values from -0.375 to 0.375
- out_weight: bfloat16 [1024, 2048], P('tp'), may hold values from -0.1875 to 0.1875
- segment_start: int32 [32768], P('seq'), may hold values from 0 to 32640, as said below
- token_valid: int32 [32768], P('seq'), may hold values from 0 to 1, as said below
- page_slot: int32 [256], P('seq'), may hold values from 4 to 511, as said below
Outputs:
- hidden: bfloat16 [32768, 2048], P('seq', 'tp')
- cache: bfloat16 [512, 128, 2048], P('seq', None, 'tp')
Inputs may be any that keep to these rules, and one draw needn't show every extreme that they name: `segment_start`: prompts start at multiples of 128 and are contiguous; each holds at most 8192 tokens and one holds exactly 8192. `token_valid`: zeros form a tail of the last page of a prompt; the first token of every prompt is 1. No two pages share a cache page; page_slot // 8 is the device that holds the page's tokens, or the next device when that one holds tokens of the same prompt. `query_weight`: independent entries whose scale falls as the inverse square root of 2048. `key_weight`: independent entries whose scale falls as the inverse square root of 2048.
All inputs are finite; a program needn't handle non-finite values.
Results may differ from a plain program's by a relative error of at most 0.02.
The roundings to bfloat16 on the way count: a program that leaves them out, or rounds other values in their place, can miss the bound.
Values may be sent and summed in bfloat16 or wider, within the bound.
No kernel may reach another device: no remote copies, remote signals or barrier semaphores. Data moves between devices by JAX's collectives and lax.ppermute only.
A program may use at most 128 MiB of HBM per device.

v0:
```python
import jax
import jax.numpy as jnp
from jax import lax
from jax.sharding import PartitionSpec as P

HD = 64
PAGE = 128
SPAN = 16


THETA = 130000.0
EPS = 1e-05


def passed_along(x, axis, by):
    count = lax.axis_size(axis)
    pairs = [(i, i + by) for i in range(count) if 0 <= i + by < count]
    return lax.ppermute(x, axis, pairs)


def rotate(inputs, positions):
    half_dim = inputs.shape[-1] // 2
    frequency = THETA ** (-2.0 * jnp.arange(half_dim, dtype=jnp.float32) / inputs.shape[-1])
    angles = positions.astype(jnp.float32)[:, None] * frequency[None, :]
    cosine = jnp.cos(angles)[:, None, :]
    sine_part = jnp.sin(angles)[:, None, :]
    front_half = inputs[..., :half_dim]
    back_half = inputs[..., half_dim:]
    return jnp.concatenate(
        [front_half * cosine - back_half * sine_part, back_half * cosine + front_half * sine_part],
        axis=-1,
    )


def body(
    residual,
    norm_gain,
    query_weight,
    key_weight,
    value_weight,
    out_weight,
    segment_start,
    token_valid,
    page_slot,
):
    row_count = residual.shape[0]
    local_heads = query_weight.shape[1] // HD
    gathered = lax.all_gather(residual, "tp", axis=1, tiled=True)
    widened = gathered.astype(jnp.float32)
    mean_sq = jnp.mean(widened * widened, axis=1, keepdims=True)
    normed = (widened * lax.rsqrt(mean_sq + EPS) * norm_gain[None, :]).astype(jnp.bfloat16)
    seq_rank = lax.axis_index("seq")
    first_row = seq_rank * row_count
    places = first_row + jnp.arange(row_count, dtype=jnp.int32)
    offsets = places - segment_start
    queries = jnp.dot(normed, query_weight, preferred_element_type=jnp.float32).reshape(
        row_count, local_heads, HD
    )
    queries = rotate(queries, offsets).astype(jnp.bfloat16)
    key_rot = jnp.dot(normed, key_weight, preferred_element_type=jnp.float32).reshape(
        row_count, local_heads, HD
    )
    key_rot = rotate(key_rot, offsets).astype(jnp.bfloat16)
    values = (
        jnp.dot(normed, value_weight, preferred_element_type=jnp.float32)
        .reshape(row_count, local_heads, HD)
        .astype(jnp.bfloat16)
    )
    packed = jnp.concatenate([key_rot[:, :, None, :], values[:, :, None, :]], axis=2).reshape(
        row_count, local_heads * 2 * HD
    )
    packed = jnp.where(token_valid[:, None] > 0, packed, jnp.zeros_like(packed))
    key_group = jnp.where(token_valid > 0, segment_start, -1)
    in_page = jnp.arange(row_count, dtype=jnp.int32) % PAGE
    page_rows = jnp.repeat(page_slot, PAGE) * PAGE + in_page
    slot_count = 2 * page_slot.shape[0]
    cache_size = slot_count * PAGE
    base_row = seq_rank * cache_size
    score_scale = HD ** (-0.5)

    def attend_block(running, incoming, allowed):
        row_max, norm_sum, weighted = running
        key_value = incoming[0].reshape(incoming[0].shape[0], local_heads, 2, HD)
        scores = (
            jnp.einsum(
                "qhd,khd->hqk", queries, key_value[:, :, 0, :], preferred_element_type=jnp.float32
            )
            * score_scale
        )
        block_max = jnp.max(jnp.where(allowed[None], scores, -1e30), axis=2)
        new_max = jnp.maximum(row_max, block_max)
        weights = jnp.where(allowed[None], jnp.exp(scores - new_max[:, :, None]), 0.0)
        shrink = jnp.exp(row_max - new_max)
        norm_sum = norm_sum * shrink + jnp.sum(weights, axis=2)
        update = jnp.einsum(
            "hqk,khd->qhd",
            weights.astype(jnp.bfloat16),
            key_value[:, :, 1, :],
            preferred_element_type=jnp.float32,
        )
        weighted = weighted * jnp.transpose(shrink)[:, :, None] + update
        return (new_max, norm_sum, weighted)

    def absorb(carried, incoming, begin_row):
        row_max, norm_sum, weighted, cache_rows = carried
        key_count = incoming[0].shape[0]
        key_places = begin_row + jnp.arange(key_count, dtype=jnp.int32)
        allowed = (
            (incoming[1][None, :] == segment_start[:, None])
            & (key_places[None, :] <= places[:, None])
            & (key_places[None, :] >= 0)
        )
        local_dest = incoming[2] - base_row
        in_range = (local_dest >= 0) & (local_dest < cache_size) & (key_places >= 0)
        target = jnp.where(in_range, local_dest, cache_size)
        cache_rows = cache_rows.at[target].set(incoming[0], mode="drop")
        running = attend_block((row_max, norm_sum, weighted), incoming, allowed)
        return (running[0], running[1], running[2], cache_rows)

    initial = (
        jnp.full((local_heads, row_count), -1e30, jnp.float32),
        jnp.zeros((local_heads, row_count), jnp.float32),
        jnp.zeros((row_count, local_heads, HD), jnp.float32),
        jnp.zeros((cache_size, local_heads * 2 * HD), jnp.bfloat16),
    )
    own_block = (packed, key_group, page_rows)
    carried = absorb(initial, own_block, first_row)
    reach_dev = min(SPAN, lax.axis_size("seq") // 2)

    def advance(step_index, carry_in):
        moving, carry_state = carry_in
        moving = passed_along((moving[0], moving[1], moving[2]), "seq", 1)
        carry_state = absorb(carry_state, moving, first_row - (step_index + 1) * row_count)
        return (moving, carry_state)

    moving, carried = lax.fori_loop(0, reach_dev, advance, (own_block, carried))
    row_max, norm_sum, weighted, cache_rows = carried
    attended = (
        (weighted / jnp.transpose(norm_sum)[:, :, None])
        .astype(jnp.bfloat16)
        .reshape(row_count, local_heads * HD)
    )
    projected = jnp.dot(attended, out_weight, preferred_element_type=jnp.float32)
    summed = lax.psum_scatter(
        projected.astype(jnp.bfloat16), "tp", scatter_dimension=1, tiled=True
    ).astype(jnp.float32)
    hidden = (residual.astype(jnp.float32) + summed).astype(jnp.bfloat16)
    return (hidden, cache_rows.reshape(slot_count, PAGE, local_heads * 2 * HD))


def solution(mesh):
    return jax.shard_map(
        body,
        mesh=mesh,
        in_specs=(
            P("seq", "tp"),
            P(),
            P(None, "tp"),
            P(None, "tp"),
            P(None, "tp"),
            P("tp", None),
            P("seq"),
            P("seq"),
            P("seq"),
        ),
        out_specs=(P("seq", "tp"), P("seq", None, "tp")),
        check_vma=False,
    )
```

profile of v0, /device:TPU:24, one launch (start us, length us, event | category | flops | bytes accessed | tf_op | source)
XLA Modules:
  0.0 630.9 jit_solution(17440001359176810723)
XLA Ops:
  10.9 51.7 %all-gather.2.cloned.1.call-done = bf16[512,2048]{1,0:T(8,128)(2,1)} async-done(((bf16[512,512]{1,0:T(8,128)(2,1)}), bf16[512,2048]{1,0:T(8,128)(2,1)}) %all-gather.2.cloned.1.call-update) | async-done | bytes 2097168 | tf_op jit(solution)/shard_map/all_gather | solution.py:48
  76.9 468.4 %while.27 = (s32[]{:T(128)}, bf16[512,512]{0,1:T(8,128)(2,1)S(1)}, s32[512]{0:T(512)S(1)}, s32[512]{0:T(512)S(1)}, f32[4,512]{1,0:T(4,128)S(1)}, /*index=5*/f32[...) while((s32[]{:T(128)}, bf16[512,512]{0,1:T(8,128)(2,1)S(1)}, ...), condition=%wide.region_8.9_spmd.clone.clone, body=%wide.region_4.8_spmd.clone.clone.sunk | while | flops 281293824 | bytes 21409060 | solution.py:136
  78.9 3.5 collective-permute-start.1
  86.2 8.7 %collective-permute-done = bf16[512,512]{0,1:T(8,128)(2,1)S(1)} collective-permute-done((bf16[512,512]{0,1:T(8,128)(2,1)S(1)}, bf16[512,512]{0,1:T(8,128)(2,1)S(1)}, u32[]{:S(2)}, u32[]{:S(2)}) %collective-permute-start) | collective-permute-done | bytes 524320 | tf_op jit(solution)/shard_map/while/body/eval_jaxpr/ppermute | solution.py:18
  100.0 3.0 scatter_fusion
  108.8 3.1 collective-permute-done.1
  112.3 7.2 %collective-permute-done = bf16[512,512]{0,1:T(8,128)(2,1)S(1)} collective-permute-done((bf16[512,512]{0,1:T(8,128)(2,1)S(1)}, bf16[512,512]{0,1:T(8,128)(2,1)S(1)}, u32[]{:S(2)}, u32[]{:S(2)}) %collective-permute-start) | collective-permute-done | bytes 524320 | tf_op jit(solution)/shard_map/while/body/eval_jaxpr/ppermute | solution.py:18
  124.5 3.0 scatter_fusion
  136.8 7.2 %collective-permute-done = bf16[512,512]{0,1:T(8,128)(2,1)S(1)} collective-permute-done((bf16[512,512]{0,1:T(8,128)(2,1)S(1)}, bf16[512,512]{0,1:T(8,128)(2,1)S(1)}, u32[]{:S(2)}, u32[]{:S(2)}) %collective-permute-start) | collective-permute-done | bytes 524320 | tf_op jit(solution)/shard_map/while/body/eval_jaxpr/ppermute | solution.py:18
  149.0 3.0 scatter_fusion
  156.6 9.0 %collective-permute-start = (bf16[512,512]{0,1:T(8,128)(2,1)S(1)}, bf16[512,512]{0,1:T(8,128)(2,1)S(1)}, u32[]{:S(2)}, u32[]{:S(2)}) collective-permute-start(bf16[512,512]{0,1:T(8,128)(2,1)S(1)} %get-tuple-element.426), channel_id=1, source_target_pairs={{0,4},{4,8},{8,12},{12,16},{16,20},{20,24},{24,28},{28,32},{32,36}... | collective-permute-start | bytes 1572872 | tf_op jit(solution)/shard_map/while/body/eval_jaxpr/ppermute | solution.py:18
  166.0 3.2 collective-permute-done
  174.3 3.0 scatter_fusion
  177.3 6.9 %collective-permute-start.2 = (s32[512]{0:T(512)S(1)}, s32[512]{0:T(512)S(1)}, u32[]{:S(2)}, u32[]{:S(2)}) collective-permute-start(s32[512]{0:T(512)S(1)} %get-tuple-element.428), channel_id=1, source_target_pairs={{0,4},{4,8},{8,12},{12,16},{16,20},{20,24},{24,28},{28,32},{32,36}... | collective-permute-start | bytes 6152 | tf_op jit(solution)/shard_map/while/body/eval_jaxpr/ppermute | solution.py:18
  184.2 4.4 collective-permute-start.1
  188.6 7.7 %collective-permute-start = (bf16[512,512]{0,1:T(8,128)(2,1)S(1)}, bf16[512,512]{0,1:T(8,128)(2,1)S(1)}, u32[]{:S(2)}, u32[]{:S(2)}) collective-permute-start(bf16[512,512]{0,1:T(8,128)(2,1)S(1)} %get-tuple-element.426), channel_id=1, source_target_pairs={{0,4},{4,8},{8,12},{12,16},{16,20},{20,24},{24,28},{28,32},{32,36}... | collective-permute-start | bytes 1572872 | tf_op jit(solution)/shard_map/while/body/eval_jaxpr/ppermute | solution.py:18
  196.7 4.5 collective-permute-done
  206.2 3.0 scatter_fusion
  209.2 5.6 collective-permute-start.2
  214.8 4.4 collective-permute-start.1
  219.2 7.6 %collective-permute-start = (bf16[512,512]{0,1:T(8,128)(2,1)S(1)}, bf16[512,512]{0,1:T(8,128)(2,1)S(1)}, u32[]{:S(2)}, u32[]{:S(2)}) collective-permute-start(bf16[512,512]{0,1:T(8,128)(2,1)S(1)} %get-tuple-element.426), channel_id=1, source_target_pairs={{0,4},{4,8},{8,12},{12,16},{16,20},{20,24},{24,28},{28,32},{32,36}... | collective-permute-start | bytes 1572872 | tf_op jit(solution)/shard_map/while/body/eval_jaxpr/ppermute | solution.py:18
  227.2 4.5 collective-permute-done
  236.8 3.0 scatter_fusion
  239.8 5.5 collective-permute-start.2
  245.3 4.4 collective-permute-start.1
  249.7 7.6 %collective-permute-start = (bf16[512,512]{0,1:T(8,128)(2,1)S(1)}, bf16[512,512]{0,1:T(8,128)(2,1)S(1)}, u32[]{:S(2)}, u32[]{:S(2)}) collective-permute-start(bf16[512,512]{0,1:T(8,128)(2,1)S(1)} %get-tuple-element.426), channel_id=1, source_target_pairs={{0,4},{4,8},{8,12},{12,16},{16,20},{20,24},{24,28},{28,32},{32,36}... | collective-permute-start | bytes 1572872 | tf_op jit(solution)/shard_map/while/body/eval_jaxpr/ppermute | solution.py:18
  257.8 4.6 collective-permute-done
  270.4 5.5 collective-permute-start.2
  275.9 4.4 collective-permute-start.1
  280.3 7.6 %collective-permute-start = (bf16[512,512]{0,1:T(8,128)(2,1)S(1)}, bf16[512,512]{0,1:T(8,128)(2,1)S(1)}, u32[]{:S(2)}, u32[]{:S(2)}) collective-permute-start(bf16[512,512]{0,1:T(8,128)(2,1)S(1)} %get-tuple-element.426), channel_id=1, source_target_pairs={{0,4},{4,8},{8,12},{12,16},{16,20},{20,24},{24,28},{28,32},{32,36}... | collective-permute-start | bytes 1572872 | tf_op jit(solution)/shard_map/while/body/eval_jaxpr/ppermute | solution.py:18
  288.3 4.6 collective-permute-done
  300.9 5.5 collective-permute-start.2
  306.5 4.4 collective-permute-start.1
  310.8 7.6 %collective-permute-start = (bf16[512,512]{0,1:T(8,128)(2,1)S(1)}, bf16[512,512]{0,1:T(8,128)(2,1)S(1)}, u32[]{:S(2)}, u32[]{:S(2)}) collective-permute-start(bf16[512,512]{0,1:T(8,128)(2,1)S(1)} %get-tuple-element.426), channel_id=1, source_target_pairs={{0,4},{4,8},{8,12},{12,16},{16,20},{20,24},{24,28},{28,32},{32,36}... | collective-permute-start | bytes 1572872 | tf_op jit(solution)/shard_map/while/body/eval_jaxpr/ppermute | solution.py:18
  318.9 4.6 collective-permute-done
  331.5 5.5 collective-permute-start.2
  337.0 4.4 collective-permute-start.1
  341.4 7.6 %collective-permute-start = (bf16[512,512]{0,1:T(8,128)(2,1)S(1)}, bf16[512,512]{0,1:T(8,128)(2,1)S(1)}, u32[]{:S(2)}, u32[]{:S(2)}) collective-permute-start(bf16[512,512]{0,1:T(8,128)(2,1)S(1)} %get-tuple-element.426), channel_id=1, source_target_pairs={{0,4},{4,8},{8,12},{12,16},{16,20},{20,24},{24,28},{28,32},{32,36}... | collective-permute-start | bytes 1572872 | tf_op jit(solution)/shard_map/while/body/eval_jaxpr/ppermute | solution.py:18
  349.5 4.6 collective-permute-done
  362.0 5.5 collective-permute-start.2
  367.6 4.4 collective-permute-start.1
  372.0 7.6 %collective-permute-start = (bf16[512,512]{0,1:T(8,128)(2,1)S(1)}, bf16[512,512]{0,1:T(8,128)(2,1)S(1)}, u32[]{:S(2)}, u32[]{:S(2)}) collective-permute-start(bf16[512,512]{0,1:T(8,128)(2,1)S(1)} %get-tuple-element.426), channel_id=1, source_target_pairs={{0,4},{4,8},{8,12},{12,16},{16,20},{20,24},{24,28},{28,32},{32,36}... | collective-permute-start | bytes 1572872 | tf_op jit(solution)/shard_map/while/body/eval_jaxpr/ppermute | solution.py:18
  380.0 4.6 collective-permute-done
  392.6 5.5 collective-permute-start.2
  398.1 4.4 collective-permute-start.1
  402.5 7.6 %collective-permute-start = (bf16[512,512]{0,1:T(8,128)(2,1)S(1)}, bf16[512,512]{0,1:T(8,128)(2,1)S(1)}, u32[]{:S(2)}, u32[]{:S(2)}) collective-permute-start(bf16[512,512]{0,1:T(8,128)(2,1)S(1)} %get-tuple-element.426), channel_id=1, source_target_pairs={{0,4},{4,8},{8,12},{12,16},{16,20},{20,24},{24,28},{28,32},{32,36}... | collective-permute-start | bytes 1572872 | tf_op jit(solution)/shard_map/while/body/eval_jaxpr/ppermute | solution.py:18
  410.6 4.6 collective-permute-done
  423.2 5.5 collective-permute-start.2
  428.7 4.4 collective-permute-start.1
  433.1 7.6 %collective-permute-start = (bf16[512,512]{0,1:T(8,128)(2,1)S(1)}, bf16[512,512]{0,1:T(8,128)(2,1)S(1)}, u32[]{:S(2)}, u32[]{:S(2)}) collective-permute-start(bf16[512,512]{0,1:T(8,128)(2,1)S(1)} %get-tuple-element.426), channel_id=1, source_target_pairs={{0,4},{4,8},{8,12},{12,16},{16,20},{20,24},{24,28},{28,32},{32,36}... | collective-permute-start | bytes 1572872 | tf_op jit(solution)/shard_map/while/body/eval_jaxpr/ppermute | solution.py:18
  441.1 4.6 collective-permute-done
  453.7 5.5 collective-permute-start.2
  459.3 4.4 collective-permute-start.1
  463.6 7.6 %collective-permute-start = (bf16[512,512]{0,1:T(8,128)(2,1)S(1)}, bf16[512,512]{0,1:T(8,128)(2,1)S(1)}, u32[]{:S(2)}, u32[]{:S(2)}) collective-permute-start(bf16[512,512]{0,1:T(8,128)(2,1)S(1)} %get-tuple-element.426), channel_id=1, source_target_pairs={{0,4},{4,8},{8,12},{12,16},{16,20},{20,24},{24,28},{28,32},{32,36}... | collective-permute-start | bytes 1572872 | tf_op jit(solution)/shard_map/while/body/eval_jaxpr/ppermute | solution.py:18
  471.7 4.6 collective-permute-done
  484.3 5.5 collective-permute-start.2
  489.8 4.4 collective-permute-start.1
  494.2 7.6 %collective-permute-start = (bf16[512,512]{0,1:T(8,128)(2,1)S(1)}, bf16[512,512]{0,1:T(8,128)(2,1)S(1)}, u32[]{:S(2)}, u32[]{:S(2)}) collective-permute-start(bf16[512,512]{0,1:T(8,128)(2,1)S(1)} %get-tuple-element.426), channel_id=1, source_target_pairs={{0,4},{4,8},{8,12},{12,16},{16,20},{20,24},{24,28},{28,32},{32,36}... | collective-permute-start | bytes 1572872 | tf_op jit(solution)/shard_map/while/body/eval_jaxpr/ppermute | solution.py:18
  502.3 4.6 collective-permute-done
  514.8 5.5 collective-permute-start.2
  520.4 4.4 collective-permute-start.1
  524.8 7.6 %collective-permute-start = (bf16[512,512]{0,1:T(8,128)(2,1)S(1)}, bf16[512,512]{0,1:T(8,128)(2,1)S(1)}, u32[]{:S(2)}, u32[]{:S(2)}) collective-permute-start(bf16[512,512]{0,1:T(8,128)(2,1)S(1)} %get-tuple-element.426), channel_id=1, source_target_pairs={{0,4},{4,8},{8,12},{12,16},{16,20},{20,24},{24,28},{28,32},{32,36}... | collective-permute-start | bytes 1572872 | tf_op jit(solution)/shard_map/while/body/eval_jaxpr/ppermute | solution.py:18
  532.8 4.6 collective-permute-done
  549.0 73.1 %reduce-scatter.2.cloned.1.call-done = bf16[512,512]{1,0:T(8,128)(2,1)} async-done(((bf16[512,2048]{1,0:T(8,128)(2,1)}), bf16[512,512]{1,0:T(8,128)(2,1)}) %reduce-scatter.2.cloned.1.call-update) | async-done | bytes 524304 | tf_op jit(solution)/shard_map/reduce_scatter | solution.py:144
  (324 shorter events, 163.3 us)
Async XLA Ops:
  7.2 539.7 %copy-start = (bf16[256,2048]{1,0:T(8,128)(2,1)S(1)}, bf16[256,2048]{1,0:T(8,128)(2,1)}, u32[]{:S(2)}) copy-start(bf16[256,2048]{1,0:T(8,128)(2,1)} %param.16) | copy-start | bytes 3145732
  7.2 60.4 %copy-start.7 = (f32[2048]{0:T(1024)S(1)}, f32[2048]{0:T(1024)}, u32[]{:S(2)}) copy-start(f32[2048]{0:T(1024)} %param.12) | copy-start | bytes 24580
  7.2 60.4 %copy-start.5 = (bf16[2048,256]{1,0:T(8,128)(2,1)S(1)}, bf16[2048,256]{1,0:T(8,128)(2,1)}, u32[]{:S(2)}) copy-start(bf16[2048,256]{1,0:T(8,128)(2,1)} %param.13) | copy-start | bytes 3145732
  7.2 55.3 %all-gather.2.cloned.1.call-start = ((), (), s32[]{:S(2)}) async-start(), calls=%async_computation.1 | async-start | bytes 2621440 | tf_op jit(solution)/shard_map/all_gather | solution.py:48
  7.9 614.2 %reduce-scatter.2.cloned.1.call-start = ((), (), s32[]{:S(2)}) async-start(), calls=%async_computation.2 | async-start | bytes 2621440 | tf_op jit(solution)/shard_map/reduce_scatter | solution.py:144
  62.5 5.1 copy-start.3
  67.6 1.2 copy-start.6
  71.8 5.1 copy-start.4
  77.0 8.9 %collective-permute-start.2 = (s32[512]{0:T(512)S(1)}, s32[512]{0:T(512)S(1)}, u32[]{:S(2)}, u32[]{:S(2)}) collective-permute-start(s32[512]{0:T(512)S(1)} %get-tuple-element.428), channel_id=1, source_target_pairs={{0,4},{4,8},{8,12},{12,16},{16,20},{20,24},{24,28},{28,32},{32,36}... | collective-permute-start | bytes 6152 | tf_op jit(solution)/shard_map/while/body/eval_jaxpr/ppermute | solution.py:18
  78.9 7.0 %collective-permute-start.1 = (s32[512]{0:T(512)S(1)}, s32[512]{0:T(512)S(1)}, u32[]{:S(2)}, u32[]{:S(2)}) collective-permute-start(s32[512]{0:T(512)S(1)} %get-tuple-element.427), channel_id=1, source_target_pairs={{0,4},{4,8},{8,12},{12,16},{16,20},{20,24},{24,28},{28,32},{32,36}... | collective-permute-start | bytes 6152 | tf_op jit(solution)/shard_map/while/body/eval_jaxpr/ppermute | solution.py:18
  82.4 12.6 %collective-permute-start = (bf16[512,512]{0,1:T(8,128)(2,1)S(1)}, bf16[512,512]{0,1:T(8,128)(2,1)S(1)}, u32[]{:S(2)}, u32[]{:S(2)}) collective-permute-start(bf16[512,512]{0,1:T(8,128)(2,1)S(1)} %get-tuple-element.426), channel_id=1, source_target_pairs={{0,4},{4,8},{8,12},{12,16},{16,20},{20,24},{24,28},{28,32},{32,36}... | collective-permute-start | bytes 1572872 | tf_op jit(solution)/shard_map/while/body/eval_jaxpr/ppermute | solution.py:18
  103.0 8.9 %collective-permute-start.2 = (s32[512]{0:T(512)S(1)}, s32[512]{0:T(512)S(1)}, u32[]{:S(2)}, u32[]{:S(2)}) collective-permute-start(s32[512]{0:T(512)S(1)} %get-tuple-element.428), channel_id=1, source_target_pairs={{0,4},{4,8},{8,12},{12,16},{16,20},{20,24},{24,28},{28,32},{32,36}... | collective-permute-start | bytes 6152 | tf_op jit(solution)/shard_map/while/body/eval_jaxpr/ppermute | solution.py:18
  104.9 7.0 %collective-permute-start.1 = (s32[512]{0:T(512)S(1)}, s32[512]{0:T(512)S(1)}, u32[]{:S(2)}, u32[]{:S(2)}) collective-permute-start(s32[512]{0:T(512)S(1)} %get-tuple-element.427), channel_id=1, source_target_pairs={{0,4},{4,8},{8,12},{12,16},{16,20},{20,24},{24,28},{28,32},{32,36}... | collective-permute-start | bytes 6152 | tf_op jit(solution)/shard_map/while/body/eval_jaxpr/ppermute | solution.py:18
  106.9 12.6 %collective-permute-start = (bf16[512,512]{0,1:T(8,128)(2,1)S(1)}, bf16[512,512]{0,1:T(8,128)(2,1)S(1)}, u32[]{:S(2)}, u32[]{:S(2)}) collective-permute-start(bf16[512,512]{0,1:T(8,128)(2,1)S(1)} %get-tuple-element.426), channel_id=1, source_target_pairs={{0,4},{4,8},{8,12},{12,16},{16,20},{20,24},{24,28},{28,32},{32,36}... | collective-permute-start | bytes 1572872 | tf_op jit(solution)/shard_map/while/body/eval_jaxpr/ppermute | solution.py:18
  127.5 8.9 %collective-permute-start.2 = (s32[512]{0:T(512)S(1)}, s32[512]{0:T(512)S(1)}, u32[]{:S(2)}, u32[]{:S(2)}) collective-permute-start(s32[512]{0:T(512)S(1)} %get-tuple-element.428), channel_id=1, source_target_pairs={{0,4},{4,8},{8,12},{12,16},{16,20},{20,24},{24,28},{28,32},{32,36}... | collective-permute-start | bytes 6152 | tf_op jit(solution)/shard_map/while/body/eval_jaxpr/ppermute | solution.py:18
  129.4 7.0 %collective-permute-start.1 = (s32[512]{0:T(512)S(1)}, s32[512]{0:T(512)S(1)}, u32[]{:S(2)}, u32[]{:S(2)}) collective-permute-start(s32[512]{0:T(512)S(1)} %get-tuple-element.427), channel_id=1, source_target_pairs={{0,4},{4,8},{8,12},{12,16},{16,20},{20,24},{24,28},{28,32},{32,36}... | collective-permute-start | bytes 6152 | tf_op jit(solution)/shard_map/while/body/eval_jaxpr/ppermute | solution.py:18
  131.3 12.6 %collective-permute-start = (bf16[512,512]{0,1:T(8,128)(2,1)S(1)}, bf16[512,512]{0,1:T(8,128)(2,1)S(1)}, u32[]{:S(2)}, u32[]{:S(2)}) collective-permute-start(bf16[512,512]{0,1:T(8,128)(2,1)S(1)} %get-tuple-element.426), channel_id=1, source_target_pairs={{0,4},{4,8},{8,12},{12,16},{16,20},{20,24},{24,28},{28,32},{32,36}... | collective-permute-start | bytes 1572872 | tf_op jit(solution)/shard_map/while/body/eval_jaxpr/ppermute | solution.py:18
  152.0 13.7 %collective-permute-start.2 = (s32[512]{0:T(512)S(1)}, s32[512]{0:T(512)S(1)}, u32[]{:S(2)}, u32[]{:S(2)}) collective-permute-start(s32[512]{0:T(512)S(1)} %get-tuple-element.428), channel_id=1, source_target_pairs={{0,4},{4,8},{8,12},{12,16},{16,20},{20,24},{24,28},{28,32},{32,36}... | collective-permute-start | bytes 6152 | tf_op jit(solution)/shard_map/while/body/eval_jaxpr/ppermute | solution.py:18
  153.9 11.8 %collective-permute-start.1 = (s32[512]{0:T(512)S(1)}, s32[512]{0:T(512)S(1)}, u32[]{:S(2)}, u32[]{:S(2)}) collective-permute-start(s32[512]{0:T(512)S(1)} %get-tuple-element.427), channel_id=1, source_target_pairs={{0,4},{4,8},{8,12},{12,16},{16,20},{20,24},{24,28},{28,32},{32,36}... | collective-permute-start | bytes 6152 | tf_op jit(solution)/shard_map/while/body/eval_jaxpr/ppermute | solution.py:18
  156.6 12.6 %collective-permute-start = (bf16[512,512]{0,1:T(8,128)(2,1)S(1)}, bf16[512,512]{0,1:T(8,128)(2,1)S(1)}, u32[]{:S(2)}, u32[]{:S(2)}) collective-permute-start(bf16[512,512]{0,1:T(8,128)(2,1)S(1)} %get-tuple-element.426), channel_id=1, source_target_pairs={{0,4},{4,8},{8,12},{12,16},{16,20},{20,24},{24,28},{28,32},{32,36}... | collective-permute-start | bytes 1572872 | tf_op jit(solution)/shard_map/while/body/eval_jaxpr/ppermute | solution.py:18
  177.3 19.0 %collective-permute-start.2 = (s32[512]{0:T(512)S(1)}, s32[512]{0:T(512)S(1)}, u32[]{:S(2)}, u32[]{:S(2)}) collective-permute-start(s32[512]{0:T(512)S(1)} %get-tuple-element.428), channel_id=1, source_target_pairs={{0,4},{4,8},{8,12},{12,16},{16,20},{20,24},{24,28},{28,32},{32,36}... | collective-permute-start | bytes 6152 | tf_op jit(solution)/shard_map/while/body/eval_jaxpr/ppermute | solution.py:18
  184.2 12.1 %collective-permute-start.1 = (s32[512]{0:T(512)S(1)}, s32[512]{0:T(512)S(1)}, u32[]{:S(2)}, u32[]{:S(2)}) collective-permute-start(s32[512]{0:T(512)S(1)} %get-tuple-element.427), channel_id=1, source_target_pairs={{0,4},{4,8},{8,12},{12,16},{16,20},{20,24},{24,28},{28,32},{32,36}... | collective-permute-start | bytes 6152 | tf_op jit(solution)/shard_map/while/body/eval_jaxpr/ppermute | solution.py:18
  188.6 12.6 %collective-permute-start = (bf16[512,512]{0,1:T(8,128)(2,1)S(1)}, bf16[512,512]{0,1:T(8,128)(2,1)S(1)}, u32[]{:S(2)}, u32[]{:S(2)}) collective-permute-start(bf16[512,512]{0,1:T(8,128)(2,1)S(1)} %get-tuple-element.426), channel_id=1, source_target_pairs={{0,4},{4,8},{8,12},{12,16},{16,20},{20,24},{24,28},{28,32},{32,36}... | collective-permute-start | bytes 1572872 | tf_op jit(solution)/shard_map/while/body/eval_jaxpr/ppermute | solution.py:18
  209.2 17.7 %collective-permute-start.2 = (s32[512]{0:T(512)S(1)}, s32[512]{0:T(512)S(1)}, u32[]{:S(2)}, u32[]{:S(2)}) collective-permute-start(s32[512]{0:T(512)S(1)} %get-tuple-element.428), channel_id=1, source_target_pairs={{0,4},{4,8},{8,12},{12,16},{16,20},{20,24},{24,28},{28,32},{32,36}... | collective-permute-start | bytes 6152 | tf_op jit(solution)/shard_map/while/body/eval_jaxpr/ppermute | solution.py:18
  214.8 12.1 %collective-permute-start.1 = (s32[512]{0:T(512)S(1)}, s32[512]{0:T(512)S(1)}, u32[]{:S(2)}, u32[]{:S(2)}) collective-permute-start(s32[512]{0:T(512)S(1)} %get-tuple-element.427), channel_id=1, source_target_pairs={{0,4},{4,8},{8,12},{12,16},{16,20},{20,24},{24,28},{28,32},{32,36}... | collective-permute-start | bytes 6152 | tf_op jit(solution)/shard_map/while/body/eval_jaxpr/ppermute | solution.py:18
  219.2 12.6 %collective-permute-start = (bf16[512,512]{0,1:T(8,128)(2,1)S(1)}, bf16[512,512]{0,1:T(8,128)(2,1)S(1)}, u32[]{:S(2)}, u32[]{:S(2)}) collective-permute-start(bf16[512,512]{0,1:T(8,128)(2,1)S(1)} %get-tuple-element.426), channel_id=1, source_target_pairs={{0,4},{4,8},{8,12},{12,16},{16,20},{20,24},{24,28},{28,32},{32,36}... | collective-permute-start | bytes 1572872 | tf_op jit(solution)/shard_map/while/body/eval_jaxpr/ppermute | solution.py:18
  239.8 17.6 %collective-permute-start.2 = (s32[512]{0:T(512)S(1)}, s32[512]{0:T(512)S(1)}, u32[]{:S(2)}, u32[]{:S(2)}) collective-permute-start(s32[512]{0:T(512)S(1)} %get-tuple-element.428), channel_id=1, source_target_pairs={{0,4},{4,8},{8,12},{12,16},{16,20},{20,24},{24,28},{28,32},{32,36}... | collective-permute-start | bytes 6152 | tf_op jit(solution)/shard_map/while/body/eval_jaxpr/ppermute | solution.py:18
  245.3 12.1 %collective-permute-start.1 = (s32[512]{0:T(512)S(1)}, s32[512]{0:T(512)S(1)}, u32[]{:S(2)}, u32[]{:S(2)}) collective-permute-start(s32[512]{0:T(512)S(1)} %get-tuple-element.427), channel_id=1, source_target_pairs={{0,4},{4,8},{8,12},{12,16},{16,20},{20,24},{24,28},{28,32},{32,36}... | collective-permute-start | bytes 6152 | tf_op jit(solution)/shard_map/while/body/eval_jaxpr/ppermute | solution.py:18
  249.7 12.6 %collective-permute-start = (bf16[512,512]{0,1:T(8,128)(2,1)S(1)}, bf16[512,512]{0,1:T(8,128)(2,1)S(1)}, u32[]{:S(2)}, u32[]{:S(2)}) collective-permute-start(bf16[512,512]{0,1:T(8,128)(2,1)S(1)} %get-tuple-element.426), channel_id=1, source_target_pairs={{0,4},{4,8},{8,12},{12,16},{16,20},{20,24},{24,28},{28,32},{32,36}... | collective-permute-start | bytes 1572872 | tf_op jit(solution)/shard_map/while/body/eval_jaxpr/ppermute | solution.py:18
  270.4 17.6 %collective-permute-start.2 = (s32[512]{0:T(512)S(1)}, s32[512]{0:T(512)S(1)}, u32[]{:S(2)}, u32[]{:S(2)}) collective-permute-start(s32[512]{0:T(512)S(1)} %get-tuple-element.428), channel_id=1, source_target_pairs={{0,4},{4,8},{8,12},{12,16},{16,20},{20,24},{24,28},{28,32},{32,36}... | collective-permute-start | bytes 6152 | tf_op jit(solution)/shard_map/while/body/eval_jaxpr/ppermute | solution.py:18
  275.9 12.1 %collective-permute-start.1 = (s32[512]{0:T(512)S(1)}, s32[512]{0:T(512)S(1)}, u32[]{:S(2)}, u32[]{:S(2)}) collective-permute-start(s32[512]{0:T(512)S(1)} %get-tuple-element.427), channel_id=1, source_target_pairs={{0,4},{4,8},{8,12},{12,16},{16,20},{20,24},{24,28},{28,32},{32,36}... | collective-permute-start | bytes 6152 | tf_op jit(solution)/shard_map/while/body/eval_jaxpr/ppermute | solution.py:18
  280.3 12.6 %collective-permute-start = (bf16[512,512]{0,1:T(8,128)(2,1)S(1)}, bf16[512,512]{0,1:T(8,128)(2,1)S(1)}, u32[]{:S(2)}, u32[]{:S(2)}) collective-permute-start(bf16[512,512]{0,1:T(8,128)(2,1)S(1)} %get-tuple-element.426), channel_id=1, source_target_pairs={{0,4},{4,8},{8,12},{12,16},{16,20},{20,24},{24,28},{28,32},{32,36}... | collective-permute-start | bytes 1572872 | tf_op jit(solution)/shard_map/while/body/eval_jaxpr/ppermute | solution.py:18
  300.9 17.6 %collective-permute-start.2 = (s32[512]{0:T(512)S(1)}, s32[512]{0:T(512)S(1)}, u32[]{:S(2)}, u32[]{:S(2)}) collective-permute-start(s32[512]{0:T(512)S(1)} %get-tuple-element.428), channel_id=1, source_target_pairs={{0,4},{4,8},{8,12},{12,16},{16,20},{20,24},{24,28},{28,32},{32,36}... | collective-permute-start | bytes 6152 | tf_op jit(solution)/shard_map/while/body/eval_jaxpr/ppermute | solution.py:18
  306.5 12.1 %collective-permute-start.1 = (s32[512]{0:T(512)S(1)}, s32[512]{0:T(512)S(1)}, u32[]{:S(2)}, u32[]{:S(2)}) collective-permute-start(s32[512]{0:T(512)S(1)} %get-tuple-element.427), channel_id=1, source_target_pairs={{0,4},{4,8},{8,12},{12,16},{16,20},{20,24},{24,28},{28,32},{32,36}... | collective-permute-start | bytes 6152 | tf_op jit(solution)/shard_map/while/body/eval_jaxpr/ppermute | solution.py:18
  310.8 12.6 %collective-permute-start = (bf16[512,512]{0,1:T(8,128)(2,1)S(1)}, bf16[512,512]{0,1:T(8,128)(2,1)S(1)}, u32[]{:S(2)}, u32[]{:S(2)}) collective-permute-start(bf16[512,512]{0,1:T(8,128)(2,1)S(1)} %get-tuple-element.426), channel_id=1, source_target_pairs={{0,4},{4,8},{8,12},{12,16},{16,20},{20,24},{24,28},{28,32},{32,36}... | collective-permute-start | bytes 1572872 | tf_op jit(solution)/shard_map/while/body/eval_jaxpr/ppermute | solution.py:18
  331.5 17.6 %collective-permute-start.2 = (s32[512]{0:T(512)S(1)}, s32[512]{0:T(512)S(1)}, u32[]{:S(2)}, u32[]{:S(2)}) collective-permute-start(s32[512]{0:T(512)S(1)} %get-tuple-element.428), channel_id=1, source_target_pairs={{0,4},{4,8},{8,12},{12,16},{16,20},{20,24},{24,28},{28,32},{32,36}... | collective-permute-start | bytes 6152 | tf_op jit(solution)/shard_map/while/body/eval_jaxpr/ppermute | solution.py:18
  337.0 12.1 %collective-permute-start.1 = (s32[512]{0:T(512)S(1)}, s32[512]{0:T(512)S(1)}, u32[]{:S(2)}, u32[]{:S(2)}) collective-permute-start(s32[512]{0:T(512)S(1)} %get-tuple-element.427), channel_id=1, source_target_pairs={{0,4},{4,8},{8,12},{12,16},{16,20},{20,24},{24,28},{28,32},{32,36}... | collective-permute-start | bytes 6152 | tf_op jit(solution)/shard_map/while/body/eval_jaxpr/ppermute | solution.py:18
  341.4 12.6 %collective-permute-start = (bf16[512,512]{0,1:T(8,128)(2,1)S(1)}, bf16[512,512]{0,1:T(8,128)(2,1)S(1)}, u32[]{:S(2)}, u32[]{:S(2)}) collective-permute-start(bf16[512,512]{0,1:T(8,128)(2,1)S(1)} %get-tuple-element.426), channel_id=1, source_target_pairs={{0,4},{4,8},{8,12},{12,16},{16,20},{20,24},{24,28},{28,32},{32,36}... | collective-permute-start | bytes 1572872 | tf_op jit(solution)/shard_map/while/body/eval_jaxpr/ppermute | solution.py:18
  362.0 17.6 %collective-permute-start.2 = (s32[512]{0:T(512)S(1)}, s32[512]{0:T(512)S(1)}, u32[]{:S(2)}, u32[]{:S(2)}) collective-permute-start(s32[512]{0:T(512)S(1)} %get-tuple-element.428), channel_id=1, source_target_pairs={{0,4},{4,8},{8,12},{12,16},{16,20},{20,24},{24,28},{28,32},{32,36}... | collective-permute-start | bytes 6152 | tf_op jit(solution)/shard_map/while/body/eval_jaxpr/ppermute | solution.py:18
  367.6 12.1 %collective-permute-start.1 = (s32[512]{0:T(512)S(1)}, s32[512]{0:T(512)S(1)}, u32[]{:S(2)}, u32[]{:S(2)}) collective-permute-start(s32[512]{0:T(512)S(1)} %get-tuple-element.427), channel_id=1, source_target_pairs={{0,4},{4,8},{8,12},{12,16},{16,20},{20,24},{24,28},{28,32},{32,36}... | collective-permute-start | bytes 6152 | tf_op jit(solution)/shard_map/while/body/eval_jaxpr/ppermute | solution.py:18
  372.0 12.6 %collective-permute-start = (bf16[512,512]{0,1:T(8,128)(2,1)S(1)}, bf16[512,512]{0,1:T(8,128)(2,1)S(1)}, u32[]{:S(2)}, u32[]{:S(2)}) collective-permute-start(bf16[512,512]{0,1:T(8,128)(2,1)S(1)} %get-tuple-element.426), channel_id=1, source_target_pairs={{0,4},{4,8},{8,12},{12,16},{16,20},{20,24},{24,28},{28,32},{32,36}... | collective-permute-start | bytes 1572872 | tf_op jit(solution)/shard_map/while/body/eval_jaxpr/ppermute | solution.py:18
  392.6 17.6 %collective-permute-start.2 = (s32[512]{0:T(512)S(1)}, s32[512]{0:T(512)S(1)}, u32[]{:S(2)}, u32[]{:S(2)}) collective-permute-start(s32[512]{0:T(512)S(1)} %get-tuple-element.428), channel_id=1, source_target_pairs={{0,4},{4,8},{8,12},{12,16},{16,20},{20,24},{24,28},{28,32},{32,36}... | collective-permute-start | bytes 6152 | tf_op jit(solution)/shard_map/while/body/eval_jaxpr/ppermute | solution.py:18
  398.1 12.1 %collective-permute-start.1 = (s32[512]{0:T(512)S(1)}, s32[512]{0:T(512)S(1)}, u32[]{:S(2)}, u32[]{:S(2)}) collective-permute-start(s32[512]{0:T(512)S(1)} %get-tuple-element.427), channel_id=1, source_target_pairs={{0,4},{4,8},{8,12},{12,16},{16,20},{20,24},{24,28},{28,32},{32,36}... | collective-permute-start | bytes 6152 | tf_op jit(solution)/shard_map/while/body/eval_jaxpr/ppermute | solution.py:18
  402.5 12.6 %collective-permute-start = (bf16[512,512]{0,1:T(8,128)(2,1)S(1)}, bf16[512,512]{0,1:T(8,128)(2,1)S(1)}, u32[]{:S(2)}, u32[]{:S(2)}) collective-permute-start(bf16[512,512]{0,1:T(8,128)(2,1)S(1)} %get-tuple-element.426), channel_id=1, source_target_pairs={{0,4},{4,8},{8,12},{12,16},{16,20},{20,24},{24,28},{28,32},{32,36}... | collective-permute-start | bytes 1572872 | tf_op jit(solution)/shard_map/while/body/eval_jaxpr/ppermute | solution.py:18
  423.2 17.6 %collective-permute-start.2 = (s32[512]{0:T(512)S(1)}, s32[512]{0:T(512)S(1)}, u32[]{:S(2)}, u32[]{:S(2)}) collective-permute-start(s32[512]{0:T(512)S(1)} %get-tuple-element.428), channel_id=1, source_target_pairs={{0,4},{4,8},{8,12},{12,16},{16,20},{20,24},{24,28},{28,32},{32,36}... | collective-permute-start | bytes 6152 | tf_op jit(solution)/shard_map/while/body/eval_jaxpr/ppermute | solution.py:18
  428.7 12.1 %collective-permute-start.1 = (s32[512]{0:T(512)S(1)}, s32[512]{0:T(512)S(1)}, u32[]{:S(2)}, u32[]{:S(2)}) collective-permute-start(s32[512]{0:T(512)S(1)} %get-tuple-element.427), channel_id=1, source_target_pairs={{0,4},{4,8},{8,12},{12,16},{16,20},{20,24},{24,28},{28,32},{32,36}... | collective-permute-start | bytes 6152 | tf_op jit(solution)/shard_map/while/body/eval_jaxpr/ppermute | solution.py:18
  433.1 12.6 %collective-permute-start = (bf16[512,512]{0,1:T(8,128)(2,1)S(1)}, bf16[512,512]{0,1:T(8,128)(2,1)S(1)}, u32[]{:S(2)}, u32[]{:S(2)}) collective-permute-start(bf16[512,512]{0,1:T(8,128)(2,1)S(1)} %get-tuple-element.426), channel_id=1, source_target_pairs={{0,4},{4,8},{8,12},{12,16},{16,20},{20,24},{24,28},{28,32},{32,36}... | collective-permute-start | bytes 1572872 | tf_op jit(solution)/shard_map/while/body/eval_jaxpr/ppermute | solution.py:18
  453.7 17.6 %collective-permute-start.2 = (s32[512]{0:T(512)S(1)}, s32[512]{0:T(512)S(1)}, u32[]{:S(2)}, u32[]{:S(2)}) collective-permute-start(s32[512]{0:T(512)S(1)} %get-tuple-element.428), channel_id=1, source_target_pairs={{0,4},{4,8},{8,12},{12,16},{16,20},{20,24},{24,28},{28,32},{32,36}... | collective-permute-start | bytes 6152 | tf_op jit(solution)/shard_map/while/body/eval_jaxpr/ppermute | solution.py:18
  459.3 12.1 %collective-permute-start.1 = (s32[512]{0:T(512)S(1)}, s32[512]{0:T(512)S(1)}, u32[]{:S(2)}, u32[]{:S(2)}) collective-permute-start(s32[512]{0:T(512)S(1)} %get-tuple-element.427), channel_id=1, source_target_pairs={{0,4},{4,8},{8,12},{12,16},{16,20},{20,24},{24,28},{28,32},{32,36}... | collective-permute-start | bytes 6152 | tf_op jit(solution)/shard_map/while/body/eval_jaxpr/ppermute | solution.py:18
  463.6 12.6 %collective-permute-start = (bf16[512,512]{0,1:T(8,128)(2,1)S(1)}, bf16[512,512]{0,1:T(8,128)(2,1)S(1)}, u32[]{:S(2)}, u32[]{:S(2)}) collective-permute-start(bf16[512,512]{0,1:T(8,128)(2,1)S(1)} %get-tuple-element.426), channel_id=1, source_target_pairs={{0,4},{4,8},{8,12},{12,16},{16,20},{20,24},{24,28},{28,32},{32,36}... | collective-permute-start | bytes 1572872 | tf_op jit(solution)/shard_map/while/body/eval_jaxpr/ppermute | solution.py:18
  484.3 17.6 %collective-permute-start.2 = (s32[512]{0:T(512)S(1)}, s32[512]{0:T(512)S(1)}, u32[]{:S(2)}, u32[]{:S(2)}) collective-permute-start(s32[512]{0:T(512)S(1)} %get-tuple-element.428), channel_id=1, source_target_pairs={{0,4},{4,8},{8,12},{12,16},{16,20},{20,24},{24,28},{28,32},{32,36}... | collective-permute-start | bytes 6152 | tf_op jit(solution)/shard_map/while/body/eval_jaxpr/ppermute | solution.py:18
  489.8 12.1 %collective-permute-start.1 = (s32[512]{0:T(512)S(1)}, s32[512]{0:T(512)S(1)}, u32[]{:S(2)}, u32[]{:S(2)}) collective-permute-start(s32[512]{0:T(512)S(1)} %get-tuple-element.427), channel_id=1, source_target_pairs={{0,4},{4,8},{8,12},{12,16},{16,20},{20,24},{24,28},{28,32},{32,36}... | collective-permute-start | bytes 6152 | tf_op jit(solution)/shard_map/while/body/eval_jaxpr/ppermute | solution.py:18
  494.2 12.6 %collective-permute-start = (bf16[512,512]{0,1:T(8,128)(2,1)S(1)}, bf16[512,512]{0,1:T(8,128)(2,1)S(1)}, u32[]{:S(2)}, u32[]{:S(2)}) collective-permute-start(bf16[512,512]{0,1:T(8,128)(2,1)S(1)} %get-tuple-element.426), channel_id=1, source_target_pairs={{0,4},{4,8},{8,12},{12,16},{16,20},{20,24},{24,28},{28,32},{32,36}... | collective-permute-start | bytes 1572872 | tf_op jit(solution)/shard_map/while/body/eval_jaxpr/ppermute | solution.py:18
  514.8 17.6 %collective-permute-start.2 = (s32[512]{0:T(512)S(1)}, s32[512]{0:T(512)S(1)}, u32[]{:S(2)}, u32[]{:S(2)}) collective-permute-start(s32[512]{0:T(512)S(1)} %get-tuple-element.428), channel_id=1, source_target_pairs={{0,4},{4,8},{8,12},{12,16},{16,20},{20,24},{24,28},{28,32},{32,36}... | collective-permute-start | bytes 6152 | tf_op jit(solution)/shard_map/while/body/eval_jaxpr/ppermute | solution.py:18
  520.4 12.1 %collective-permute-start.1 = (s32[512]{0:T(512)S(1)}, s32[512]{0:T(512)S(1)}, u32[]{:S(2)}, u32[]{:S(2)}) collective-permute-start(s32[512]{0:T(512)S(1)} %get-tuple-element.427), channel_id=1, source_target_pairs={{0,4},{4,8},{8,12},{12,16},{16,20},{20,24},{24,28},{28,32},{32,36}... | collective-permute-start | bytes 6152 | tf_op jit(solution)/shard_map/while/body/eval_jaxpr/ppermute | solution.py:18
  524.8 12.6 %collective-permute-start = (bf16[512,512]{0,1:T(8,128)(2,1)S(1)}, bf16[512,512]{0,1:T(8,128)(2,1)S(1)}, u32[]{:S(2)}, u32[]{:S(2)}) collective-permute-start(bf16[512,512]{0,1:T(8,128)(2,1)S(1)} %get-tuple-element.426), channel_id=1, source_target_pairs={{0,4},{4,8},{8,12},{12,16},{16,20},{20,24},{24,28},{28,32},{32,36}... | collective-permute-start | bytes 1572872 | tf_op jit(solution)/shard_map/while/body/eval_jaxpr/ppermute | solution.py:18
  545.4 78.7 %copy-start.1 = (bf16[1024,512]{1,0:T(8,128)(2,1)}, bf16[1024,512]{1,0:T(8,128)(2,1)S(1)}, u32[]{:S(2)}) copy-start(bf16[1024,512]{1,0:T(8,128)(2,1)S(1)} %get-tuple-element.220) | copy-start | bytes 3145732
  545.4 76.7 %copy-start.2 = (bf16[512,512]{1,0:T(8,128)(2,1)S(1)}, bf16[512,512]{1,0:T(8,128)(2,1)}, u32[]{:S(2)}) copy-start(bf16[512,512]{1,0:T(8,128)(2,1)} %param.11) | copy-start | bytes 1572868
Sparse Core Ops, SparseCore 0:
  9.8 52.6 all-gather.1
  549.1 72.9 reduce-scatter.1
where the time goes:
time: 634 us; the launch traced here: 631 us
  starting transfers between devices  245 us (39%)
  waiting for transfers between devices  214 us (34%)
  matrix products  70.6 us (11%)
  local copies, waits for them, and re-layouts  54.7 us (9%)
  other arithmetic  30.1 us (5%)
  between operations  14.3 us (2%)
    ppermute x48, starting transfers between devices, passed_along(): return lax.ppermute(x, axis, pairs)  245 us
    ppermute x48, waiting for transfers between devices, passed_along(): return lax.ppermute(x, axis, pairs)  88.6 us
    reduce_scatter x1, waiting for transfers between devices, body(): lax.psum_scatter(projected.astype(jnp.bfloat16), 'tp', scatter_dimension=...  73.1 us
    all_gather x1, waiting for transfers between devices, body(): gathered = lax.all_gather(residual, 'tp', axis=1, tiled=True)  51.7 us
    scatter x17, local copies, waits for them, and re-layouts, absorb(): cache_rows = cache_rows.at[target].set(incoming[0], mode='drop')  50.2 us
    dot_general x17, matrix products, attend_block(): jnp.einsum('hqk,khd->qhd', weights.astype(jnp.bfloat16), key_value[:, :,...  48.3 us
    reduce_sum x17, other arithmetic, attend_block(): norm_sum = norm_sum * shrink + jnp.sum(weights, axis=2)  15.5 us
    dot_general x17, matrix products, attend_block(): jnp.einsum('qhd,khd->hqk', queries, key_value[:, :, 0, :], preferred_elem...  15.5 us
  transfers between devices with their start and end apart: 50, of which 21 were waited for; matrix products, arithmetic and copies ran while one was open for 1% of the time, Pallas kernels for 0%

commit v1 on v0

--- a/solution.py
+++ b/solution.py
@@ -70,17 +70,14 @@
         row_count, local_heads * 2 * HD
     )
     packed = jnp.where(token_valid[:, None] > 0, packed, jnp.zeros_like(packed))
-    key_group = jnp.where(token_valid > 0, segment_start, -1)
-    in_page = jnp.arange(row_count, dtype=jnp.int32) % PAGE
-    page_rows = jnp.repeat(page_slot, PAGE) * PAGE + in_page
-    slot_count = 2 * page_slot.shape[0]
-    cache_size = slot_count * PAGE
-    base_row = seq_rank * cache_size
     score_scale = HD ** (-0.5)
+
+    out_cols = lax.all_to_all(out_weight, "tp", 1, 0, tiled=True)
+    prev_slot = passed_along(page_slot, "seq", 1)
 
     def attend_block(running, incoming, allowed):
         row_max, norm_sum, weighted = running
-        key_value = incoming[0].reshape(incoming[0].shape[0], local_heads, 2, HD)
+        key_value = incoming.reshape(incoming.shape[0], local_heads, 2, HD)
         scores = (
             jnp.einsum(
                 "qhd,khd->hqk", queries, key_value[:, :, 0, :], preferred_element_type=jnp.float32
@@ -101,51 +98,59 @@
         weighted = weighted * jnp.transpose(shrink)[:, :, None] + update
         return (new_max, norm_sum, weighted)
 
-    def absorb(carried, incoming, begin_row):
-        row_max, norm_sum, weighted, cache_rows = carried
-        key_count = incoming[0].shape[0]
-        key_places = begin_row + jnp.arange(key_count, dtype=jnp.int32)
-        allowed = (
-            (incoming[1][None, :] == segment_start[:, None])
-            & (key_places[None, :] <= places[:, None])
-            & (key_places[None, :] >= 0)
-        )
-        local_dest = incoming[2] - base_row
-        in_range = (local_dest >= 0) & (local_dest < cache_size) & (key_places >= 0)
-        target = jnp.where(in_range, local_dest, cache_size)
-        cache_rows = cache_rows.at[target].set(incoming[0], mode="drop")
-        running = attend_block((row_max, norm_sum, weighted), incoming, allowed)
-        return (running[0], running[1], running[2], cache_rows)
-
+    local_pos = jnp.arange(row_count, dtype=jnp.int32)
+    own_allowed = (
+        ((first_row + local_pos)[None, :] >= segment_start[:, None])
+        & (local_pos[None, :] <= local_pos[:, None])
+        & (token_valid[None, :] > 0)
+    )
     initial = (
         jnp.full((local_heads, row_count), -1e30, jnp.float32),
         jnp.zeros((local_heads, row_count), jnp.float32),
         jnp.zeros((row_count, local_heads, HD), jnp.float32),
-        jnp.zeros((cache_size, local_heads * 2 * HD), jnp.bfloat16),
     )
-    own_block = (packed, key_group, page_rows)
-    carried = absorb(initial, own_block, first_row)
+    carried = attend_block(initial, packed, own_allowed)
+
+    def remote_absorb(running, incoming, step):
+        key_places = first_row - step * row_count + local_pos
+        allowed = key_places[None, :] >= segment_start[:, None]
+        return attend_block(running, incoming, allowed)
+
+    prev_block = passed_along(packed, "seq", 1)
+    carried = remote_absorb(carried, prev_block, 1)
     reach_dev = min(SPAN, lax.axis_size("seq") // 2)
 
     def advance(step_index, carry_in):
-        moving, carry_state = carry_in
-        moving = passed_along((moving[0], moving[1], moving[2]), "seq", 1)
-        carry_state = absorb(carry_state, moving, first_row - (step_index + 1) * row_count)
-        return (moving, carry_state)
+        moving, running = carry_in
+        moving = passed_along(moving, "seq", 1)
+        running = remote_absorb(running, moving, step_index)
+        return (moving, running)
 
-    moving, carried = lax.fori_loop(0, reach_dev, advance, (own_block, carried))
-    row_max, norm_sum, weighted, cache_rows = carried
+    _, carried = lax.fori_loop(2, reach_dev + 1, advance, (prev_block, carried))
+    row_max, norm_sum, weighted = carried
     attended = (
         (weighted / jnp.transpose(norm_sum)[:, :, None])
         .astype(jnp.bfloat16)
         .reshape(row_count, local_heads * HD)
     )
-    projected = jnp.dot(attended, out_weight, preferred_element_type=jnp.float32)
-    summed = lax.psum_scatter(
-        projected.astype(jnp.bfloat16), "tp", scatter_dimension=1, tiled=True
-    ).astype(jnp.float32)
-    hidden = (residual.astype(jnp.float32) + summed).astype(jnp.bfloat16)
-    return (hidden, cache_rows.reshape(slot_count, PAGE, local_heads * 2 * HD))
+
+    tiles = page_slot.shape[0]
+    slot_count = 2 * tiles
+    base_slot = seq_rank * slot_count
+    has_prev = seq_rank > 0
+    cand_slot = jnp.concatenate([page_slot, jnp.where(has_prev, prev_slot, -1)]) - base_slot
+    cand_pages = jnp.concatenate(
+        [packed.reshape(tiles, PAGE, -1), prev_block.reshape(tiles, PAGE, -1)], axis=0
+    )
+    match = cand_slot[None, :] == jnp.arange(slot_count, dtype=jnp.int32)[:, None]
+    pick = jnp.argmax(match.astype(jnp.int32), axis=1)
+    found = jnp.any(match, axis=1)
+    cache_pages = jnp.where(found[:, None, None], cand_pages[pick], jnp.zeros_like(cand_pages[:1]))
+
+    attended_all = lax.all_gather(attended, "tp", axis=1, tiled=True)
+    projected = jnp.dot(attended_all, out_cols, preferred_element_type=jnp.float32)
+    hidden = (residual.astype(jnp.float32) + projected).astype(jnp.bfloat16)
+    return (hidden, cache_pages)
 
 
 def solution(mesh):

time: 634 us -> 501 us (0.79)
  starting transfers between devices: 245 us -> 56.7 us
  waiting for transfers between devices: 214 us -> 327 us
  local copies, waits for them, and re-layouts: 54.7 us -> 22.4 us
  matrix products: 70.6 us -> 46.4 us
    ppermute x48 -> x17, starting transfers between devices: 245 us -> 50.8 us  [passed_along(): return lax.ppermute(x, axis, pairs)]
    all_gather x0 -> x1, waiting for transfers between devices: none -> 121 us  [body(): attended_all = lax.all_gather(attended, 'tp', axis=1, tiled=True)]
    reduce_scatter x1 -> x0, waiting for transfers between devices: 73.1 us -> none  [body(): lax.psum_scatter(projected.astype(jnp.bfloat16), 'tp', scatter_dimension=...]
    ppermute x48 -> x17, waiting for transfers between devices: 88.6 us -> 152 us  [passed_along(): return lax.ppermute(x, axis, pairs)]
    scatter x17 -> x0, local copies, waits for them, and re-layouts: 50.2 us -> none  [absorb(): cache_rows = cache_rows.at[target].set(incoming[0], mode='drop')]
    dot_general x17, matrix products: 48.3 us -> 19.7 us  [attend_block(): jnp.einsum('hqk,khd->qhd', weights.astype(jnp.bfloat16), key_value[:, :,...]
    while x64 -> x90, local copies, waits for them, and re-layouts: 0.69 us -> 14.6 us
  transfers between devices with their start and end apart: 50 -> 20, of which waited for: 21 -> 18; matrix products, arithmetic and copies ran while one was open for 1% -> 19% of each run, Pallas kernels for 0% -> 0%
where the time goes in v1:
time: 501 us; the launch traced here: 500 us
  waiting for transfers between devices  327 us (65%)
  starting transfers between devices  56.7 us (11%)
  matrix products  46.4 us (9%)
  other arithmetic  31.1 us (6%)
  local copies, waits for them, and re-layouts  22.4 us (4%)
  between operations  14.4 us (3%)
    ppermute x17, waiting for transfers between devices, passed_along(): return lax.ppermute(x, axis, pairs)  152 us
    all_gather x1, waiting for transfers between devices, body(): attended_all = lax.all_gather(attended, 'tp', axis=1, tiled=True)  121 us
    all_gather x1, waiting for transfers between devices, body(): gathered = lax.all_gather(residual, 'tp', axis=1, tiled=True)  53.8 us
    ppermute x17, starting transfers between devices, passed_along(): return lax.ppermute(x, axis, pairs)  50.8 us
    dot_general x17, matrix products, attend_block(): jnp.einsum('hqk,khd->qhd', weights.astype(jnp.bfloat16), key_value[:, :,...  19.7 us
    dot_general x17, matrix products, attend_block(): jnp.einsum('qhd,khd->hqk', queries, key_value[:, :, 0, :], preferred_elem...  17.8 us
    reduce_sum x17, other arithmetic, attend_block(): norm_sum = norm_sum * shrink + jnp.sum(weights, axis=2)  15.4 us
    while x90, local copies, waits for them, and re-layouts  14.6 us
  transfers between devices with their start and end apart: 20, of which 18 were waited for; matrix products, arithmetic and copies ran while one was open for 19% of the time, Pallas kernels for 0%

profile of v1, /device:TPU:24, one launch (start us, length us, event | category | flops | bytes accessed | tf_op | source)
XLA Modules:
  0.0 499.8 jit_solution(5178662731228044125)
XLA Ops:
  8.0 2.3 copy.46
  10.2 5.9 %all-to-all-start = ((bf16[256,4,512]{0,2,1:T(8,128)(2,1)}), bf16[256,4,512]{0,2,1:T(8,128)(2,1)S(1)}, u32[]{:S(2)}, u32[]{:S(2)}) async-start(bf16[256,4,512]{0,2,1:T(8,128)(2,1)} %bitcast.17), calls=%async_computation | async-start | bytes 2097152 | tf_op jit(solution)/shard_map/all_to_all | solution.py:75
  16.1 1.9 collective-permute-start.2
  18.4 1.2 fusion.47
  19.6 53.8 %all-gather.3.cloned.1.call-done = bf16[512,2048]{1,0:T(8,128)(2,1)} async-done(((bf16[512,512]{1,0:T(8,128)(2,1)}), bf16[512,2048]{1,0:T(8,128)(2,1)}) %all-gather.3.cloned.1.call-update) | async-done | bytes 2097168 | tf_op jit(solution)/shard_map/all_gather | solution.py:48
  73.4 2.2 fusion.17
  75.7 2.5 fusion.64
  78.2 2.3 fusion.61
  84.1 2.1 collective-permute-start.1
  87.1 2.0 select_reduce_fusion.2
  89.2 7.7 %collective-permute-done.1 = bf16[512,512]{0,1:T(8,128)(2,1)S(1)} collective-permute-done((bf16[512,512]{0,1:T(8,128)(2,1)}, bf16[512,512]{0,1:T(8,128)(2,1)S(1)}, u32[]{:S(2)}, u32[]{:S(2)}) %collective-permute-start.1) | collective-permute-done | bytes 524320 | tf_op jit(solution)/shard_map/ppermute | solution.py:18
  96.9 2.1 select_reduce_fusion.1
  102.0 1.8 fusion.37
  104.7 254.9 %while.20 = (s32[]{:T(128)}, bf16[512,512]{0,1:T(8,128)(2,1)}, f32[4,512]{1,0:T(4,128)S(1)}, f32[4,512]{1,0:T(4,128)S(1)}, f32[512,4,64]{0,2,1:T(8,128)}, /*inde...) while((s32[]{:T(128)}, bf16[512,512]{0,1:T(8,128)(2,1)}, ...), condition=%wide.region_8.9_spmd.clone, body=%wide.region_5.8_spmd.clone.sunk | while | flops 280500736 | bytes 22943988 | solution.py:129
  104.7 1.9 collective-permute-start
  106.8 10.7 %collective-permute-done = bf16[512,512]{0,1:T(8,128)(2,1)S(1)} collective-permute-done((bf16[512,512]{0,1:T(8,128)(2,1)}, bf16[512,512]{0,1:T(8,128)(2,1)S(1)}, u32[]{:S(2)}, u32[]{:S(2)}) %collective-permute-start) | collective-permute-done | bytes 524320 | tf_op jit(solution)/shard_map/while/body/eval_jaxpr/ppermute | solution.py:18
  119.4 1.1 fusion.82
  121.5 1.9 collective-permute-start
  123.6 10.7 %collective-permute-done = bf16[512,512]{0,1:T(8,128)(2,1)S(1)} collective-permute-done((bf16[512,512]{0,1:T(8,128)(2,1)}, bf16[512,512]{0,1:T(8,128)(2,1)S(1)}, u32[]{:S(2)}, u32[]{:S(2)}) %collective-permute-start) | collective-permute-done | bytes 524320 | tf_op jit(solution)/shard_map/while/body/eval_jaxpr/ppermute | solution.py:18
  136.2 1.1 fusion.82
  138.3 1.9 collective-permute-start
  140.4 10.7 %collective-permute-done = bf16[512,512]{0,1:T(8,128)(2,1)S(1)} collective-permute-done((bf16[512,512]{0,1:T(8,128)(2,1)}, bf16[512,512]{0,1:T(8,128)(2,1)S(1)}, u32[]{:S(2)}, u32[]{:S(2)}) %collective-permute-start) | collective-permute-done | bytes 524320 | tf_op jit(solution)/shard_map/while/body/eval_jaxpr/ppermute | solution.py:18
  153.0 1.1 fusion.82
  155.1 1.9 collective-permute-start
  157.2 10.7 %collective-permute-done = bf16[512,512]{0,1:T(8,128)(2,1)S(1)} collective-permute-done((bf16[512,512]{0,1:T(8,128)(2,1)}, bf16[512,512]{0,1:T(8,128)(2,1)S(1)}, u32[]{:S(2)}, u32[]{:S(2)}) %collective-permute-start) | collective-permute-done | bytes 524320 | tf_op jit(solution)/shard_map/while/body/eval_jaxpr/ppermute | solution.py:18
  169.8 1.1 fusion.82
  171.9 1.9 collective-permute-start
  174.0 10.7 %collective-permute-done = bf16[512,512]{0,1:T(8,128)(2,1)S(1)} collective-permute-done((bf16[512,512]{0,1:T(8,128)(2,1)}, bf16[512,512]{0,1:T(8,128)(2,1)S(1)}, u32[]{:S(2)}, u32[]{:S(2)}) %collective-permute-start) | collective-permute-done | bytes 524320 | tf_op jit(solution)/shard_map/while/body/eval_jaxpr/ppermute | solution.py:18
  186.6 1.1 fusion.82
  188.7 1.9 collective-permute-start
  190.8 10.7 %collective-permute-done = bf16[512,512]{0,1:T(8,128)(2,1)S(1)} collective-permute-done((bf16[512,512]{0,1:T(8,128)(2,1)}, bf16[512,512]{0,1:T(8,128)(2,1)S(1)}, u32[]{:S(2)}, u32[]{:S(2)}) %collective-permute-start) | collective-permute-done | bytes 524320 | tf_op jit(solution)/shard_map/while/body/eval_jaxpr/ppermute | solution.py:18
  203.4 1.1 fusion.82
  205.5 1.9 collective-permute-start
  207.6 10.7 %collective-permute-done = bf16[512,512]{0,1:T(8,128)(2,1)S(1)} collective-permute-done((bf16[512,512]{0,1:T(8,128)(2,1)}, bf16[512,512]{0,1:T(8,128)(2,1)S(1)}, u32[]{:S(2)}, u32[]{:S(2)}) %collective-permute-start) | collective-permute-done | bytes 524320 | tf_op jit(solution)/shard_map/while/body/eval_jaxpr/ppermute | solution.py:18
  220.2 1.1 fusion.82
  222.3 1.9 collective-permute-start
  224.4 10.7 %collective-permute-done = bf16[512,512]{0,1:T(8,128)(2,1)S(1)} collective-permute-done((bf16[512,512]{0,1:T(8,128)(2,1)}, bf16[512,512]{0,1:T(8,128)(2,1)S(1)}, u32[]{:S(2)}, u32[]{:S(2)}) %collective-permute-start) | collective-permute-done | bytes 524320 | tf_op jit(solution)/shard_map/while/body/eval_jaxpr/ppermute | solution.py:18
  237.0 1.1 fusion.82
  239.1 1.9 collective-permute-start
  241.2 10.7 %collective-permute-done = bf16[512,512]{0,1:T(8,128)(2,1)S(1)} collective-permute-done((bf16[512,512]{0,1:T(8,128)(2,1)}, bf16[512,512]{0,1:T(8,128)(2,1)S(1)}, u32[]{:S(2)}, u32[]{:S(2)}) %collective-permute-start) | collective-permute-done | bytes 524320 | tf_op jit(solution)/shard_map/while/body/eval_jaxpr/ppermute | solution.py:18
  253.8 1.1 fusion.82
  255.9 1.9 collective-permute-start
  258.0 10.7 %collective-permute-done = bf16[512,512]{0,1:T(8,128)(2,1)S(1)} collective-permute-done((bf16[512,512]{0,1:T(8,128)(2,1)}, bf16[512,512]{0,1:T(8,128)(2,1)S(1)}, u32[]{:S(2)}, u32[]{:S(2)}) %collective-permute-start) | collective-permute-done | bytes 524320 | tf_op jit(solution)/shard_map/while/body/eval_jaxpr/ppermute | solution.py:18
  270.6 1.1 fusion.82
  272.7 1.9 collective-permute-start
  274.8 10.7 %collective-permute-done = bf16[512,512]{0,1:T(8,128)(2,1)S(1)} collective-permute-done((bf16[512,512]{0,1:T(8,128)(2,1)}, bf16[512,512]{0,1:T(8,128)(2,1)S(1)}, u32[]{:S(2)}, u32[]{:S(2)}) %collective-permute-start) | collective-permute-done | bytes 524320 | tf_op jit(solution)/shard_map/while/body/eval_jaxpr/ppermute | solution.py:18
  287.4 1.1 fusion.82
  289.5 1.9 collective-permute-start
  291.6 10.7 %collective-permute-done = bf16[512,512]{0,1:T(8,128)(2,1)S(1)} collective-permute-done((bf16[512,512]{0,1:T(8,128)(2,1)}, bf16[512,512]{0,1:T(8,128)(2,1)S(1)}, u32[]{:S(2)}, u32[]{:S(2)}) %collective-permute-start) | collective-permute-done | bytes 524320 | tf_op jit(solution)/shard_map/while/body/eval_jaxpr/ppermute | solution.py:18
  304.2 1.1 fusion.82
  306.3 1.9 collective-permute-start
  308.4 10.6 %collective-permute-done = bf16[512,512]{0,1:T(8,128)(2,1)S(1)} collective-permute-done((bf16[512,512]{0,1:T(8,128)(2,1)}, bf16[512,512]{0,1:T(8,128)(2,1)S(1)}, u32[]{:S(2)}, u32[]{:S(2)}) %collective-permute-start) | collective-permute-done | bytes 524320 | tf_op jit(solution)/shard_map/while/body/eval_jaxpr/ppermute | solution.py:18
  321.0 1.1 fusion.82
  323.1 8.0 %collective-permute-start = (bf16[512,512]{0,1:T(8,128)(2,1)}, bf16[512,512]{0,1:T(8,128)(2,1)S(1)}, u32[]{:S(2)}, u32[]{:S(2)}) collective-permute-start(bf16[512,512]{0,1:T(8,128)(2,1)} %get-tuple-element.290), channel_id=1, source_target_pairs={{0,4},{4,8},{8,12},{12,16},{16,20},{20,24},{24,28},{28,32},{32,36}... | collective-permute-start | bytes 1572872 | tf_op jit(solution)/shard_map/while/body/eval_jaxpr/ppermute | solution.py:18
  331.3 4.6 collective-permute-done
  337.8 1.1 fusion.82
  339.9 14.0 %collective-permute-start = (bf16[512,512]{0,1:T(8,128)(2,1)}, bf16[512,512]{0,1:T(8,128)(2,1)S(1)}, u32[]{:S(2)}, u32[]{:S(2)}) collective-permute-start(bf16[512,512]{0,1:T(8,128)(2,1)} %get-tuple-element.290), channel_id=1, source_target_pairs={{0,4},{4,8},{8,12},{12,16},{16,20},{20,24},{24,28},{28,32},{32,36}... | collective-permute-start | bytes 1572872 | tf_op jit(solution)/shard_map/while/body/eval_jaxpr/ppermute | solution.py:18
  354.1 1.5 collective-permute-done
  357.4 1.1 fusion.82
  359.5 1.8 divide_convert_fusion
  362.9 1.3 copy.47
  365.9 1.3 copy.50
  369.0 120.7 %all-gather.5.cloned.1.call-done = bf16[512,1024]{0,1:T(8,128)(2,1)} async-done(((bf16[512,256]{0,1:T(8,128)(2,1)}), bf16[512,1024]{0,1:T(8,128)(2,1)}) %all-gather.5.cloned.1.call-update) | async-done | bytes 1048592 | tf_op jit(solution)/shard_map/all_gather | solution.py:150
  489.7 3.2 fusion.30
  (240 shorter events, 59.8 us)
Async XLA Ops:
  7.2 68.5 %copy-start = (bf16[2048,256]{1,0:T(8,128)(2,1)S(1)}, bf16[2048,256]{1,0:T(8,128)(2,1)}, u32[]{:S(2)}) copy-start(bf16[2048,256]{1,0:T(8,128)(2,1)} %param.14) | copy-start | bytes 3145732
  7.2 8.9 %copy-start.10 = (s32[4]{0:T(128)S(1)}, s32[4]{0:T(128)}, u32[]{:S(2)}) copy-start(s32[4]{0:T(128)} %param.19) | copy-start | bytes 52
  7.2 10.9 %copy-start.9 = (s32[512]{0:T(512)S(1)}, s32[512]{0:T(512)}, u32[]{:S(2)}) copy-start(s32[512]{0:T(512)} %param.18) | copy-start | bytes 6148
  7.2 10.9 %copy-start.8 = (s32[512]{0:T(512)S(1)}, s32[512]{0:T(512)}, u32[]{:S(2)}) copy-start(s32[512]{0:T(512)} %param.17) | copy-start | bytes 6148
  7.2 68.4 %copy-start.12 = (f32[2048]{0:T(1024)S(1)}, f32[2048]{0:T(1024)}, u32[]{:S(2)}) copy-start(f32[2048]{0:T(1024)} %param.12) | copy-start | bytes 24580
  7.2 66.2 %all-gather.3.cloned.1.call-start = ((), (), s32[]{:S(2)}) async-start(), calls=%async_computation.1 | async-start | bytes 2621440 | tf_op jit(solution)/shard_map/all_gather | solution.py:48
  10.2 352.7 %all-to-all-start = ((bf16[256,4,512]{0,2,1:T(8,128)(2,1)}), bf16[256,4,512]{0,2,1:T(8,128)(2,1)S(1)}, u32[]{:S(2)}, u32[]{:S(2)}) async-start(bf16[256,4,512]{0,2,1:T(8,128)(2,1)} %bitcast.17), calls=%async_computation | async-start | bytes 2097152 | tf_op jit(solution)/shard_map/all_to_all | solution.py:75
  16.1 473.6 %all-gather.5.cloned.1.call-start = ((), (), s32[]{:S(2)}) async-start(), calls=%async_computation.2 | async-start | bytes 1310720 | tf_op jit(solution)/shard_map/all_gather | solution.py:150
  16.1 345.2 %collective-permute-start.2 = (s32[4]{0:T(128)S(1)}, s32[4]{0:T(128)}, u32[]{:S(2)}, u32[]{:S(2)}) collective-permute-start(s32[4]{0:T(128)S(1)} %copy-done.10), channel_id=1, source_target_pairs={{0,4},{4,8},{8,12},{12,16},{16,20},{20,24},{24,28},{28,32},{32,36}... | collective-permute-start | bytes 56 | tf_op jit(solution)/shard_map/ppermute | solution.py:18
  73.4 4.8 copy-start.1
  78.2 3.1 copy-start.11
  84.1 12.8 %collective-permute-start.1 = (bf16[512,512]{0,1:T(8,128)(2,1)}, bf16[512,512]{0,1:T(8,128)(2,1)S(1)}, u32[]{:S(2)}, u32[]{:S(2)}) collective-permute-start(bf16[512,512]{0,1:T(8,128)(2,1)} %bitcast_select_fusion), channel_id=1, source_target_pairs={{0,4},{4,8},{8,12},{12,16},{16,20},{20,24},{24,28},{28,32},{32,36}... | collective-permute-start | bytes 1572872 | tf_op jit(solution)/shard_map/ppermute | solution.py:18
  87.1 11.9 %copy-start.4 = (pred[512,512]{0,1:T(8,128)(4,1)S(1)}, pred[512,512]{0,1:T(8,128)(4,1)}, u32[]{:S(2)}) copy-start(pred[512,512]{0,1:T(8,128)(4,1)} %get-tuple-element.213) | copy-start | bytes 786436
  96.9 7.0 %copy-start.2 = (bf16[512,512]{0,1:T(8,128)(2,1)}, bf16[512,512]{0,1:T(8,128)(2,1)S(1)}, u32[]{:S(2)}) copy-start(bf16[512,512]{0,1:T(8,128)(2,1)S(1)} %collective-permute-done.1) | copy-start | bytes 1572868
  96.9 3.1 copy-start.7
  100.0 1.1 copy-start.3
  104.7 12.8 %collective-permute-start = (bf16[512,512]{0,1:T(8,128)(2,1)}, bf16[512,512]{0,1:T(8,128)(2,1)S(1)}, u32[]{:S(2)}, u32[]{:S(2)}) collective-permute-start(bf16[512,512]{0,1:T(8,128)(2,1)} %get-tuple-element.290), channel_id=1, source_target_pairs={{0,4},{4,8},{8,12},{12,16},{16,20},{20,24},{24,28},{28,32},{32,36}... | collective-permute-start | bytes 1572872 | tf_op jit(solution)/shard_map/while/body/eval_jaxpr/ppermute | solution.py:18
  117.5 1.9 copy-start.5
  120.5 1.0 copy-start.6
  121.5 12.8 %collective-permute-start = (bf16[512,512]{0,1:T(8,128)(2,1)}, bf16[512,512]{0,1:T(8,128)(2,1)S(1)}, u32[]{:S(2)}, u32[]{:S(2)}) collective-permute-start(bf16[512,512]{0,1:T(8,128)(2,1)} %get-tuple-element.290), channel_id=1, source_target_pairs={{0,4},{4,8},{8,12},{12,16},{16,20},{20,24},{24,28},{28,32},{32,36}... | collective-permute-start | bytes 1572872 | tf_op jit(solution)/shard_map/while/body/eval_jaxpr/ppermute | solution.py:18
  134.3 1.9 copy-start.5
  137.3 1.0 copy-start.6
  138.3 12.8 %collective-permute-start = (bf16[512,512]{0,1:T(8,128)(2,1)}, bf16[512,512]{0,1:T(8,128)(2,1)S(1)}, u32[]{:S(2)}, u32[]{:S(2)}) collective-permute-start(bf16[512,512]{0,1:T(8,128)(2,1)} %get-tuple-element.290), channel_id=1, source_target_pairs={{0,4},{4,8},{8,12},{12,16},{16,20},{20,24},{24,28},{28,32},{32,36}... | collective-permute-start | bytes 1572872 | tf_op jit(solution)/shard_map/while/body/eval_jaxpr/ppermute | solution.py:18
  151.1 1.9 copy-start.5
  154.1 1.0 copy-start.6
  155.1 12.8 %collective-permute-start = (bf16[512,512]{0,1:T(8,128)(2,1)}, bf16[512,512]{0,1:T(8,128)(2,1)S(1)}, u32[]{:S(2)}, u32[]{:S(2)}) collective-permute-start(bf16[512,512]{0,1:T(8,128)(2,1)} %get-tuple-element.290), channel_id=1, source_target_pairs={{0,4},{4,8},{8,12},{12,16},{16,20},{20,24},{24,28},{28,32},{32,36}... | collective-permute-start | bytes 1572872 | tf_op jit(solution)/shard_map/while/body/eval_jaxpr/ppermute | solution.py:18
  167.9 1.9 copy-start.5
  170.9 1.0 copy-start.6
  171.9 12.8 %collective-permute-start = (bf16[512,512]{0,1:T(8,128)(2,1)}, bf16[512,512]{0,1:T(8,128)(2,1)S(1)}, u32[]{:S(2)}, u32[]{:S(2)}) collective-permute-start(bf16[512,512]{0,1:T(8,128)(2,1)} %get-tuple-element.290), channel_id=1, source_target_pairs={{0,4},{4,8},{8,12},{12,16},{16,20},{20,24},{24,28},{28,32},{32,36}... | collective-permute-start | bytes 1572872 | tf_op jit(solution)/shard_map/while/body/eval_jaxpr/ppermute | solution.py:18
  184.7 1.9 copy-start.5
  187.7 1.0 copy-start.6
  188.7 12.8 %collective-permute-start = (bf16[512,512]{0,1:T(8,128)(2,1)}, bf16[512,512]{0,1:T(8,128)(2,1)S(1)}, u32[]{:S(2)}, u32[]{:S(2)}) collective-permute-start(bf16[512,512]{0,1:T(8,128)(2,1)} %get-tuple-element.290), channel_id=1, source_target_pairs={{0,4},{4,8},{8,12},{12,16},{16,20},{20,24},{24,28},{28,32},{32,36}... | collective-permute-start | bytes 1572872 | tf_op jit(solution)/shard_map/while/body/eval_jaxpr/ppermute | solution.py:18
  201.5 1.9 copy-start.5
  204.5 1.0 copy-start.6
  205.5 12.8 %collective-permute-start = (bf16[512,512]{0,1:T(8,128)(2,1)}, bf16[512,512]{0,1:T(8,128)(2,1)S(1)}, u32[]{:S(2)}, u32[]{:S(2)}) collective-permute-start(bf16[512,512]{0,1:T(8,128)(2,1)} %get-tuple-element.290), channel_id=1, source_target_pairs={{0,4},{4,8},{8,12},{12,16},{16,20},{20,24},{24,28},{28,32},{32,36}... | collective-permute-start | bytes 1572872 | tf_op jit(solution)/shard_map/while/body/eval_jaxpr/ppermute | solution.py:18
  218.3 1.9 copy-start.5
  221.3 1.0 copy-start.6
  222.3 12.8 %collective-permute-start = (bf16[512,512]{0,1:T(8,128)(2,1)}, bf16[512,512]{0,1:T(8,128)(2,1)S(1)}, u32[]{:S(2)}, u32[]{:S(2)}) collective-permute-start(bf16[512,512]{0,1:T(8,128)(2,1)} %get-tuple-element.290), channel_id=1, source_target_pairs={{0,4},{4,8},{8,12},{12,16},{16,20},{20,24},{24,28},{28,32},{32,36}... | collective-permute-start | bytes 1572872 | tf_op jit(solution)/shard_map/while/body/eval_jaxpr/ppermute | solution.py:18
  235.1 1.9 copy-start.5
  238.1 1.0 copy-start.6
  239.1 12.8 %collective-permute-start = (bf16[512,512]{0,1:T(8,128)(2,1)}, bf16[512,512]{0,1:T(8,128)(2,1)S(1)}, u32[]{:S(2)}, u32[]{:S(2)}) collective-permute-start(bf16[512,512]{0,1:T(8,128)(2,1)} %get-tuple-element.290), channel_id=1, source_target_pairs={{0,4},{4,8},{8,12},{12,16},{16,20},{20,24},{24,28},{28,32},{32,36}... | collective-permute-start | bytes 1572872 | tf_op jit(solution)/shard_map/while/body/eval_jaxpr/ppermute | solution.py:18
  251.9 1.9 copy-start.5
  254.9 1.0 copy-start.6
  255.9 12.8 %collective-permute-start = (bf16[512,512]{0,1:T(8,128)(2,1)}, bf16[512,512]{0,1:T(8,128)(2,1)S(1)}, u32[]{:S(2)}, u32[]{:S(2)}) collective-permute-start(bf16[512,512]{0,1:T(8,128)(2,1)} %get-tuple-element.290), channel_id=1, source_target_pairs={{0,4},{4,8},{8,12},{12,16},{16,20},{20,24},{24,28},{28,32},{32,36}... | collective-permute-start | bytes 1572872 | tf_op jit(solution)/shard_map/while/body/eval_jaxpr/ppermute | solution.py:18
  268.7 1.9 copy-start.5
  271.7 1.0 copy-start.6
  272.7 12.8 %collective-permute-start = (bf16[512,512]{0,1:T(8,128)(2,1)}, bf16[512,512]{0,1:T(8,128)(2,1)S(1)}, u32[]{:S(2)}, u32[]{:S(2)}) collective-permute-start(bf16[512,512]{0,1:T(8,128)(2,1)} %get-tuple-element.290), channel_id=1, source_target_pairs={{0,4},{4,8},{8,12},{12,16},{16,20},{20,24},{24,28},{28,32},{32,36}... | collective-permute-start | bytes 1572872 | tf_op jit(solution)/shard_map/while/body/eval_jaxpr/ppermute | solution.py:18
  285.5 1.9 copy-start.5
  288.5 1.0 copy-start.6
  289.5 12.8 %collective-permute-start = (bf16[512,512]{0,1:T(8,128)(2,1)}, bf16[512,512]{0,1:T(8,128)(2,1)S(1)}, u32[]{:S(2)}, u32[]{:S(2)}) collective-permute-start(bf16[512,512]{0,1:T(8,128)(2,1)} %get-tuple-element.290), channel_id=1, source_target_pairs={{0,4},{4,8},{8,12},{12,16},{16,20},{20,24},{24,28},{28,32},{32,36}... | collective-permute-start | bytes 1572872 | tf_op jit(solution)/shard_map/while/body/eval_jaxpr/ppermute | solution.py:18
  302.3 1.9 copy-start.5
  305.3 1.0 copy-start.6
  306.3 12.8 %collective-permute-start = (bf16[512,512]{0,1:T(8,128)(2,1)}, bf16[512,512]{0,1:T(8,128)(2,1)S(1)}, u32[]{:S(2)}, u32[]{:S(2)}) collective-permute-start(bf16[512,512]{0,1:T(8,128)(2,1)} %get-tuple-element.290), channel_id=1, source_target_pairs={{0,4},{4,8},{8,12},{12,16},{16,20},{20,24},{24,28},{28,32},{32,36}... | collective-permute-start | bytes 1572872 | tf_op jit(solution)/shard_map/while/body/eval_jaxpr/ppermute | solution.py:18
  319.1 1.9 copy-start.5
  322.1 1.0 copy-start.6
  323.1 12.8 %collective-permute-start = (bf16[512,512]{0,1:T(8,128)(2,1)}, bf16[512,512]{0,1:T(8,128)(2,1)S(1)}, u32[]{:S(2)}, u32[]{:S(2)}) collective-permute-start(bf16[512,512]{0,1:T(8,128)(2,1)} %get-tuple-element.290), channel_id=1, source_target_pairs={{0,4},{4,8},{8,12},{12,16},{16,20},{20,24},{24,28},{28,32},{32,36}... | collective-permute-start | bytes 1572872 | tf_op jit(solution)/shard_map/while/body/eval_jaxpr/ppermute | solution.py:18
  335.9 1.9 copy-start.5
  338.9 1.0 copy-start.6
  339.9 15.7 %collective-permute-start = (bf16[512,512]{0,1:T(8,128)(2,1)}, bf16[512,512]{0,1:T(8,128)(2,1)S(1)}, u32[]{:S(2)}, u32[]{:S(2)}) collective-permute-start(bf16[512,512]{0,1:T(8,128)(2,1)} %get-tuple-element.290), channel_id=1, source_target_pairs={{0,4},{4,8},{8,12},{12,16},{16,20},{20,24},{24,28},{28,32},{32,36}... | collective-permute-start | bytes 1572872 | tf_op jit(solution)/shard_map/while/body/eval_jaxpr/ppermute | solution.py:18
  355.6 1.9 copy-start.5
  358.6 1.0 copy-start.6
Sparse Core Ops, SparseCore 0:
  9.8 63.5 all-gather.2
  361.5 128.1 all-gather.4
